TPU v7x, 32 devices: a whole 2x2x4 slice. The times are simulated.
32 devices in a mesh: lat: 2 (over y), lev: 4 (over x, core), ocn: 4 (over z).
Axes of the slice: x: 2, y: 2, z: 4, core: 2. Of those that a mesh axis runs over, the one named last changes fastest.
Arguments:
- atmos_fields: bfloat16 [2, 24, 2560, 5632], P(None, 'lev', ('lat', 'ocn')), may hold values from -6 to 6
- lat_points: int32 [2560], P(('lat', 'ocn')), may hold values from 20 to 5632, as said below
- wave_order: int32 [32], replicated, may hold values from 0 to 31, each once
- legendre: bfloat16 [32, 2560, 1536], P(('lat', 'ocn'), None, 'lev'), may hold values from -0.125 to 0.125
- column_weight: bfloat16 [2, 24], P(None, 'lev'), may hold values from -1.25 to 1.25
- block_remap: int32 [2560, 44], P(('lat', 'ocn'), 'lev'), may hold values from 0 to 2175, as said below
- ocean_temp: float32 [128, 2176], P(('lat', 'ocn')), may hold values from -6 to 6
- ocean_salt: float32 [128, 2176], P(('lat', 'ocn')), may hold values from -6 to 6
- sea_mask: int32 [128, 17], P(('lat', 'ocn')), may hold values 0 or 1
Outputs:
- spectra: float32 [32, 96, 1536], P(('lat', 'ocn'), None, 'lev')
- temp_next: float32 [128, 2176], P(('lat', 'ocn'))
- salt_next: float32 [128, 2176], P(('lat', 'ocn'))
- surface_temp: float32 [2560, 5632], P(('lat', 'ocn'), 'lev')
Inputs may be any that keep to these rules, and one draw needn't show every extreme that they name: `lat_points`: a multiple of 4 for every latitude row. `wave_order`: each wavenumber appears once. `block_remap`: the blocks of latitude band g (rows g * 320 onward) name tiles of ocean sections g - 1, g or g + 1 only; section g holds tiles g * 16 * 17 onward, in row order.
All inputs are finite; a program needn't handle non-finite values. No bound on the sum of `sea_mask` on one device may be relied on, other than what follows from the above.
Results may differ from a plain program's by a relative error of at most 0.0037.
Values may be sent and summed in bfloat16 or wider, within the bound.
No kernel may reach another device: no remote copies, remote signals or barrier semaphores. Data moves between devices by JAX's collectives and lax.ppermute only.
A program may use at most 192 MiB of HBM per device.

v0:
```python
import math
import jax
import jax.numpy as jnp
from jax import lax
from jax.sharding import PartitionSpec as P

FIELDS = 2
BLOCK = 128
FULL_TURN = 2.0 * math.pi
DIFFUSION = 0.2
COUPLING = 0.5


def with_halo(cells, sides, width):
    for axis, dim in sides:
        count = lax.axis_size(axis)
        ends = count - 1
        head = lax.slice_in_dim(cells, 0, width, axis=dim)
        tail = lax.slice_in_dim(cells, cells.shape[dim] - width, cells.shape[dim], axis=dim)
        cells = jnp.concatenate(
            [
                lax.ppermute(tail, axis, [(i, (i + 1) % count) for i in range(ends)]),
                cells,
                lax.ppermute(head, axis, [((i + 1) % count, i) for i in range(ends)]),
            ],
            axis=dim,
        )
    return cells


def fourier_table(wave_order, length):
    points = jnp.arange(length, dtype=jnp.int32)
    phase = wave_order[None, :] * points[:, None] % length
    angle = phase.astype(jnp.float32) * (FULL_TURN / length)
    table = jnp.concatenate([jnp.cos(angle), -jnp.sin(angle)], axis=1).astype(jnp.bfloat16)
    return (table, points)


def body(
    atmos_fields,
    lat_points,
    wave_order,
    legendre,
    column_weight,
    block_remap,
    ocean_temp,
    ocean_salt,
    sea_mask,
):
    nfields, lev_dev, lat_band, lon_count = atmos_fields.shape
    wave_count = wave_order.shape[0]
    table, points = fourier_table(wave_order, lon_count)
    point_mask = points[None, :] < lat_points[:, None]
    masked = jnp.where(point_mask[None, None], atmos_fields, jnp.zeros((), jnp.bfloat16))
    inverse_root = 1.0 / jnp.sqrt(lat_points.astype(jnp.float32))
    weights = jnp.where(
        2 * wave_order[None, :] < lat_points[:, None],
        inverse_root[:, None],
        jnp.zeros((), jnp.float32),
    )
    field_count = masked.shape[0]
    raw_sums = jnp.dot(masked.reshape(-1, lon_count), table, preferred_element_type=jnp.float32)
    raw_sums = raw_sums.reshape(field_count, lev_dev, lat_band, 2, wave_count)
    coeffs = (raw_sums * weights[None, None, :, None, :]).astype(jnp.bfloat16)
    regrouped = lax.all_to_all(
        coeffs.transpose(4, 1, 0, 3, 2).reshape(wave_count, lev_dev * field_count * 2, lat_band),
        ("lat", "ocn"),
        split_axis=0,
        concat_axis=2,
        tiled=True,
    )
    spectra = jnp.einsum(
        "srj,sjd->srd",
        lax.all_gather(regrouped, "lev", axis=1, tiled=True),
        legendre,
        preferred_element_type=jnp.float32,
    )
    ocean_rows, ocean_cols = ocean_temp.shape
    tile_count = ocean_rows * ocean_cols // BLOCK
    band_index = lax.axis_index(("lat", "ocn"))

    def slot_of(targets):
        return (targets // tile_count - band_index + 1) * tile_count + targets % tile_count

    local_slot = slot_of(block_remap.reshape(-1))
    partial_sum = jnp.einsum(
        "ql,qljk->qjk", column_weight, masked, preferred_element_type=jnp.float32
    )
    quarter = lon_count // lax.axis_size("lev")
    full_remap = lax.all_gather(block_remap, "lev", axis=1, tiled=True)
    every_slot = slot_of(full_remap.reshape(-1))
    block_rows = (
        partial_sum.reshape(FIELDS, lat_band, lon_count // BLOCK, BLOCK)
        .transpose(1, 2, 0, 3)
        .reshape(-1, FIELDS * BLOCK)
    )
    outgoing = jax.ops.segment_sum(block_rows, every_slot, num_segments=3 * tile_count)
    widened = with_halo(outgoing, ((("lat", "ocn"), 0),), tile_count)
    arrived = (
        widened[:tile_count] + widened[2 * tile_count : 3 * tile_count] + widened[4 * tile_count :]
    )
    tile_sums = lax.psum(arrived, "lev")
    forcing = (
        tile_sums.reshape(ocean_rows, ocean_cols // BLOCK, FIELDS, BLOCK)
        .transpose(2, 0, 1, 3)
        .reshape(FIELDS, ocean_rows, ocean_cols)
    )
    sea_cells = (
        jnp.broadcast_to(sea_mask[:, :, None], (ocean_rows, ocean_cols // BLOCK, BLOCK))
        .reshape(ocean_rows, ocean_cols)
        .astype(jnp.float32)
    )
    ocean_state = jnp.stack([ocean_temp, ocean_salt])
    padded = with_halo(ocean_state, ((("lat", "ocn"), 1),), 1)
    laplace = (
        padded[:, 2:]
        + padded[:, :-2]
        + jnp.roll(ocean_state, 1, 2)
        + jnp.roll(ocean_state, -1, 2)
        - 4.0 * ocean_state
    )
    updated = ocean_state + DIFFUSION * laplace + COUPLING * sea_cells[None] * forcing
    temp_next = updated[0]
    salt_next = updated[1]
    returned = with_halo(temp_next, ((("lat", "ocn"), 0),), ocean_rows)
    tiles_near = returned.reshape(3 * tile_count, BLOCK)
    surface = jnp.take(tiles_near, local_slot, axis=0).reshape(lat_band, quarter)
    own_points = lax.axis_index("lev") * quarter + jnp.arange(quarter, dtype=jnp.int32)
    surface_temp = jnp.where(
        own_points[None, :] < lat_points[:, None], surface, jnp.zeros((), jnp.float32)
    )
    return (spectra, temp_next, salt_next, surface_temp)


def solution(mesh):
    placed = (
        P(None, "lev", ("lat", "ocn"), None),
        P(("lat", "ocn")),
        P(),
        P(("lat", "ocn"), None, "lev"),
        P(None, "lev"),
        P(("lat", "ocn"), "lev"),
        P(("lat", "ocn"), None),
        P(("lat", "ocn"), None),
        P(("lat", "ocn"), None),
    )
    return jax.shard_map(
        body,
        mesh=mesh,
        in_specs=placed,
        out_specs=(
            P(("lat", "ocn"), None, "lev"),
            P(("lat", "ocn"), None),
            P(("lat", "ocn"), None),
            P(("lat", "ocn"), "lev"),
        ),
        check_vma=False,
    )
```

profile of v0, /device:TPU:4, one launch (start us, length us, event | category | flops | bytes accessed | tf_op | source)
XLA Modules:
  0.0 345.3 jit_solution(12073367168310134059)
XLA Ops:
  7.2 1.7 iota_compare_fusion
  8.9 0.7 convert_rsqrt_fusion
  9.6 4.0 %cosine_convert_fusion = (bf16[5632,32]{0,1:T(8,128)(2,1)S(1)}, bf16[5632,32]{0,1:T(8,128)(2,1)S(1)}) fusion(s32[32]{0:T(128)} %param.11), kind=kLoop, calls=%fused_computation.21 | loop fusion | flops 2162688 | bytes 721024 | tf_op jit(solution)/shard_map/convert
  13.6 0.7 broadcast_multiply_fusion
  14.3 28.9 %broadcast_select_fusion = bf16[2,6,320,5632]{3,2,1,0:T(8,128)(2,1)} fusion(bf16[2,6,320,5632]{3,2,1,0:T(8,128)(2,1)} %param.9, pred[320,5632]{1,0:T(8,128)(4,1)S(1)} %iota_compare_fusion), kind=kLoop, calls=%fused_computation.6 | loop fusion | flops 21626880 | bytes 88309760 | tf_op jit(solution)/shard_map/jit(_where)/select_n | solution.py:54
  43.3 21.6 %fusion.13 = bf16[32,6,2,2,320]{4,0,3,1,2:T(8,128)(2,1)S(1)} fusion(bf16[2,32,5632,1,1]{2,1,0,4,3:T(8,128)(2,1)S(1)} %bitcast.66, bf16[2,6,320,5632]{3,2,1,0:T(8,128)(2,1)} %broadcast_select_fusion, f32[32,320]{1,0:T(8,128)S(1)} %compare_select_fusion.2), kind=kOutput, calls=%fused_computation.15 | convolution fusion | flops 2768732160 | bytes 44507136 | tf_op jit(solution)/shard_map/dot_general | solution.py:62
  65.0 1.0 copy.40
  66.0 6.3 %all-to-all-start = ((bf16[32,24,320]{2,1,0:T(8,128)(2,1)}), bf16[32,24,320]{2,1,0:T(8,128)(2,1)S(1)}, u32[]{:S(2)}, u32[]{:S(2)}) async-start(bf16[32,24,320]{2,1,0:T(8,128)(2,1)} %copy.40), calls=%async_computation | async-start | bytes 1179648 | tf_op jit(solution)/shard_map/all_to_all | solution.py:65
  72.4 5.5 %all-gather = s32[4,11,320]{2,1,0:T(8,128)S(1)} all-gather(s32[1,11,320]{2,1,0:T(8,128)S(1)} %bitcast.82), channel_id=1, replica_groups=mesh['lat'=2,'lev'=4,'ocn'=4] {'lev'}, dimensions={0}, use_global_device_ids=true | all-gather | bytes 70400 | tf_op jit(solution)/shard_map/all_gather | solution.py:90
  78.0 0.1 copy.43
  78.1 0.2 rem.67
  78.3 0.1 copy.44
  78.4 0.2 div.38
  78.7 0.1 copy.42
  78.8 0.2 ne.124
  79.0 42.8 %fusion = f32[2,1,320,5632]{3,1,2,0:T(1,128)} fusion(bf16[2,6,320,5632]{3,2,1,0:T(8,128)(2,1)} %broadcast_select_fusion, bf16[2,6,1,1]{1,0,2,3:T(2,128)(2,1)S(1)} %bitcast.62), kind=kOutput, calls=%fused_computation.2 | convolution fusion | flops 43253760 | bytes 57671704 | tf_op jit(solution)/shard_map/ql,qljk->qjk/dot_general | solution.py:86
  121.8 11.2 %copy.69 = f32[2,1,320,5632]{3,2,0,1:T(8,128)} copy(f32[2,1,320,5632]{3,1,2,0:T(1,128)} %fusion) | data formatting | bytes 28835840 | tf_op jit(solution)/shard_map/ql,qljk->qjk/dot_general | solution.py:86
  133.0 16.2 %reshape.273 = f32[2,320,44,128]{3,2,1,0:T(8,128)} reshape(f32[2,320,5632]{2,1,0:T(8,128)} %bitcast.64) | data formatting | bytes 28835840 | tf_op jit(solution)/shard_map/reshape | solution.py:93
  149.2 21.4 %copy.45 = f32[320,44,2,128]{3,2,1,0:T(2,128)} copy(f32[320,44,2,128]{3,1,0,2:T(8,128)} %bitcast.63) | data formatting | bytes 28835840 | tf_op jit(solution)/shard_map/transpose | solution.py:94
  170.6 0.4 fusion.33
  171.0 77.7 %scatter_custom_fusion = f32[816,256]{1,0:T(8,128)S(1)} fusion(s32[14080]{0:T(1024)S(1)} %fusion.33, f32[1760,8,2,128]{3,2,1,0:T(2,128)} %bitcast.65, f32[]{:T(128)} %constant.51.clone.1), kind=kCustom, calls=%fused_computation.7 | custom fusion | flops 3604480 | bytes 15253508 | tf_op jit(solution)/shard_map/scatter-add | solution.py:97
  248.8 5.4 %collective-permute-start.3 = (f32[272,256]{1,0:T(8,128)S(1)}, f32[272,256]{1,0:T(8,128)S(1)}, u32[]{:S(2)}, u32[]{:S(2)}) collective-permute-start(f32[272,256]{1,0:T(8,128)S(1)} %get-tuple-element.19), channel_id=1, source_target_pairs={{1,0},{2,1},{3,2},{16,3},{17,16},{18,17},{19,18},{5,4},{6,5},{7,6}... | collective-permute-start | bytes 835592 | tf_op jit(solution)/shard_map/ppermute | solution.py:24
  254.2 1.9 collective-permute-start.2
  256.1 2.1 collective-permute-start.1
  258.3 6.4 %collective-permute-start = (f32[2,1,2176]{2,1,0:T(1,128)S(1)}, f32[2,1,2176]{2,1,0:T(1,128)S(1)}, u32[]{:S(2)}, u32[]{:S(2)}) collective-permute-start(f32[2,1,2176]{2,1,0:T(1,128)S(1)} %get-tuple-element.26), channel_id=1, source_target_pairs={{1,0},{2,1},{3,2},{16,3},{17,16},{18,17},{19,18},{5,4},{6,5},{7,6}... | collective-permute-start | bytes 52232 | tf_op jit(solution)/shard_map/ppermute | solution.py:24
  264.7 3.1 collective-permute-done.2
  267.9 0.1 reshape.275
  268.1 0.8 reshape.276
  269.1 0.2 rem.71
  269.4 0.2 div.40
  269.7 0.2 copy.41
  269.9 1.2 all_to_all.16
  271.1 0.2 copy.47
  271.2 0.2 ne.132
  271.6 0.1 fusion.23
  272.0 29.3 %all-reduce.2.cloned.1.call-done = f32[2,16,2176]{2,1,0:T(8,128)} async-done(((f32[2,16,2176]{2,1,0:T(8,128)}), f32[2,16,2176]{2,1,0:T(8,128)}) %all-reduce.2.cloned.1.call-update) | async-done | bytes 278544 | tf_op jit(solution)/shard_map/psum | solution.py:102
  301.3 1.2 fusion.31
  302.5 0.7 slice_bitcast_fusion
  303.2 5.2 %collective-permute-start.5 = (f32[16,2176]{1,0:T(8,128)S(1)}, f32[16,2176]{1,0:T(8,128)S(1)}, u32[]{:S(2)}, u32[]{:S(2)}) collective-permute-start(f32[16,2176]{1,0:T(8,128)S(1)} %get-tuple-element.21), channel_id=1, source_target_pairs={{1,0},{2,1},{3,2},{16,3},{17,16},{18,17},{19,18},{5,4},{6,5},{7,6}... | collective-permute-start | bytes 417800 | tf_op jit(solution)/shard_map/ppermute | solution.py:24
  308.4 1.9 collective-permute-start.4
  310.4 1.9 collective-permute-done.5
  312.3 5.8 %collective-permute-done.4 = f32[16,2176]{1,0:T(8,128)S(1)} collective-permute-done((f32[16,2176]{1,0:T(8,128)S(1)}, f32[16,2176]{1,0:T(8,128)S(1)}, u32[]{:S(2)}, u32[]{:S(2)}) %collective-permute-start.4) | collective-permute-done | bytes 139296 | tf_op jit(solution)/shard_map/ppermute | solution.py:22
  318.1 5.9 %gather_fusion = f32[3520,128]{1,0:T(8,128)S(1)} fusion(f32[816,128]{1,0:T(8,128)S(1)} %reshape.277, s32[4096]{0:T(1024)S(1)} %pad_clamp_fusion), kind=kCustom, calls=%fused_computation | custom fusion | bytes 3618560 | tf_op jit(solution)/shard_map/jit(_take)/gather | solution.py:127
  324.0 1.6 gather.7
  325.6 2.2 copy.50
  327.8 1.7 select_select_fusion
  329.5 2.9 copy.51
  332.4 6.1 %fusion.46 = f32[4,96,384]{2,1,0:T(8,128)} fusion(bf16[4,96,2560]{2,1,0:T(8,128)(2,1)} %all-gather.3.cloned.1.call-done, bf16[4,2560,384]{2,1,0:T(8,128)(2,1)} %param.12), kind=kOutput, calls=%fused_computation.94 | convolution fusion | flops 754974720 | bytes 10420224 | tf_op jit(solution)/shard_map/srj,sjd->srd/dot_general | solution.py:72
  (50 shorter events, 1.3 us)
Async XLA Ops:
  7.2 71.9 %copy-start = (bf16[2,6]{1,0:T(2,128)(2,1)S(1)}, bf16[2,6]{1,0:T(2,128)(2,1)}, u32[]{:S(2)}) copy-start(bf16[2,6]{1,0:T(2,128)(2,1)} %param.13) | copy-start | bytes 76
  14.3 29.0 %copy-start.6 = (s32[320]{0:T(512)S(1)}, s32[320]{0:T(512)}, u32[]{:S(2)}) copy-start(s32[320]{0:T(512)} %param.10) | copy-start | bytes 3844
  43.3 29.0 %copy-start.5 = (s32[320,11]{0,1:T(8,128)S(1)}, s32[320,11]{0,1:T(8,128)}, u32[]{:S(2)}) copy-start(s32[320,11]{0,1:T(8,128)} %param.14) | copy-start | bytes 42244
  66.0 203.6 %all-to-all-start = ((bf16[32,24,320]{2,1,0:T(8,128)(2,1)}), bf16[32,24,320]{2,1,0:T(8,128)(2,1)S(1)}, u32[]{:S(2)}, u32[]{:S(2)}) async-start(bf16[32,24,320]{2,1,0:T(8,128)(2,1)} %copy.40), calls=%async_computation | async-start | bytes 1179648 | tf_op jit(solution)/shard_map/all_to_all | solution.py:65
  72.3 229.0 %all-reduce.2.cloned.1.call-start = ((), (), s32[]{:S(2)}) async-start(), calls=%async_computation.2 | async-start | bytes 557056 | tf_op jit(solution)/shard_map/psum | solution.py:102
  171.0 85.1 %copy-start.2 = (f32[16,2176]{1,0:T(8,128)S(1)}, f32[16,2176]{1,0:T(8,128)}, u32[]{:S(2)}) copy-start(f32[16,2176]{1,0:T(8,128)} %param.15) | copy-start | bytes 417796
  171.0 85.1 %copy-start.3 = (f32[16,2176]{1,0:T(8,128)S(1)}, f32[16,2176]{1,0:T(8,128)}, u32[]{:S(2)}) copy-start(f32[16,2176]{1,0:T(8,128)} %param.16) | copy-start | bytes 417796
  248.7 22.9 %copy-start.7 = (s32[16,17]{1,0:T(8,128)S(1)}, s32[16,17]{1,0:T(8,128)}, u32[]{:S(2)}) copy-start(s32[16,17]{1,0:T(8,128)} %param.17) | copy-start | bytes 3268
  248.8 15.9 %collective-permute-start.3 = (f32[272,256]{1,0:T(8,128)S(1)}, f32[272,256]{1,0:T(8,128)S(1)}, u32[]{:S(2)}, u32[]{:S(2)}) collective-permute-start(f32[272,256]{1,0:T(8,128)S(1)} %get-tuple-element.19), channel_id=1, source_target_pairs={{1,0},{2,1},{3,2},{16,3},{17,16},{18,17},{19,18},{5,4},{6,5},{7,6}... | collective-permute-start | bytes 835592 | tf_op jit(solution)/shard_map/ppermute | solution.py:24
  254.2 13.7 %collective-permute-start.2 = (f32[272,256]{1,0:T(8,128)S(1)}, f32[272,256]{1,0:T(8,128)S(1)}, u32[]{:S(2)}, u32[]{:S(2)}) collective-permute-start(f32[272,256]{1,0:T(8,128)S(1)} %get-tuple-element.18), channel_id=1, source_target_pairs={{0,1},{1,2},{2,3},{3,16},{16,17},{17,18},{18,19},{4,5},{5,6},{6,7}... | collective-permute-start | bytes 835592 | tf_op jit(solution)/shard_map/ppermute | solution.py:22
  256.1 15.8 %collective-permute-start.1 = (f32[2,1,2176]{2,1,0:T(1,128)S(1)}, f32[2,1,2176]{2,1,0:T(1,128)S(1)}, u32[]{:S(2)}, u32[]{:S(2)}) collective-permute-start(f32[2,1,2176]{2,1,0:T(1,128)S(1)} %get-tuple-element.27), channel_id=1, source_target_pairs={{0,1},{1,2},{2,3},{3,16},{16,17},{17,18},{18,19},{4,5},{5,6},{6,7}... | collective-permute-start | bytes 52232 | tf_op jit(solution)/shard_map/ppermute | solution.py:22
  258.3 13.7 %collective-permute-start = (f32[2,1,2176]{2,1,0:T(1,128)S(1)}, f32[2,1,2176]{2,1,0:T(1,128)S(1)}, u32[]{:S(2)}, u32[]{:S(2)}) collective-permute-start(f32[2,1,2176]{2,1,0:T(1,128)S(1)} %get-tuple-element.26), channel_id=1, source_target_pairs={{1,0},{2,1},{3,2},{16,3},{17,16},{18,17},{19,18},{5,4},{6,5},{7,6}... | collective-permute-start | bytes 52232 | tf_op jit(solution)/shard_map/ppermute | solution.py:24
  268.9 63.5 %all-gather.3.cloned.1.call-start = ((), (), s32[]{:S(2)}) async-start(), calls=%async_computation.1 | async-start | bytes 2457600 | tf_op jit(solution)/shard_map/all_gather | solution.py:74
  303.2 20.8 %copy-start.4 = (f32[16,2176]{1,0:T(8,128)}, f32[16,2176]{1,0:T(8,128)S(1)}, u32[]{:S(2)}) copy-start(f32[16,2176]{1,0:T(8,128)S(1)} %get-tuple-element.21) | copy-start | bytes 417796
  303.2 9.1 %collective-permute-start.5 = (f32[16,2176]{1,0:T(8,128)S(1)}, f32[16,2176]{1,0:T(8,128)S(1)}, u32[]{:S(2)}, u32[]{:S(2)}) collective-permute-start(f32[16,2176]{1,0:T(8,128)S(1)} %get-tuple-element.21), channel_id=1, source_target_pairs={{1,0},{2,1},{3,2},{16,3},{17,16},{18,17},{19,18},{5,4},{6,5},{7,6}... | collective-permute-start | bytes 417800 | tf_op jit(solution)/shard_map/ppermute | solution.py:24
  308.4 9.6 %collective-permute-start.4 = (f32[16,2176]{1,0:T(8,128)S(1)}, f32[16,2176]{1,0:T(8,128)S(1)}, u32[]{:S(2)}, u32[]{:S(2)}) collective-permute-start(f32[16,2176]{1,0:T(8,128)S(1)} %get-tuple-element.21), channel_id=1, source_target_pairs={{0,1},{1,2},{2,3},{3,16},{16,17},{17,18},{18,19},{4,5},{5,6},{6,7}... | collective-permute-start | bytes 417800 | tf_op jit(solution)/shard_map/ppermute | solution.py:22
  327.8 10.6 %copy-start.1 = (bf16[2,6]{1,0:T(2,128)(2,1)S(1)}, bf16[2,6]{1,0:T(2,128)(2,1)}, u32[]{:S(2)}) copy-start(bf16[2,6]{1,0:T(2,128)(2,1)} %param.13) | copy-start | bytes 76
Sparse Core Ops, SparseCore 0:
  269.0 32.3 all-reduce.1
  303.5 22.2 all-gather.2
where the time goes:
time: 346 us; the launch traced here: 345 us
  other arithmetic  118 us (34%)
  matrix products  70.5 us (20%)
  local copies, waits for them, and re-layouts  67.7 us (20%)
  waiting for transfers between devices  40.2 us (12%)
  starting transfers between devices  29.4 us (8%)
  between operations  14.5 us (4%)
  blocking collectives  5.52 us (2%)
    scatter-add x1, other arithmetic, body(): jax.ops.segment_sum(block_rows, every_slot, num_segments=3 * tile_count)  77.7 us
    dot_general x1, matrix products, body(): jnp.einsum('ql,qljk->qjk', column_weight, masked, preferred_element_type=...  42.8 us
    psum x1, waiting for transfers between devices, body(): tile_sums = lax.psum(arrived, 'lev')  29.3 us
    select_n x1, other arithmetic, body(): jnp.where(point_mask[None, None], atmos_fields, jnp.zeros((), jnp.bfloat16))  28.9 us
    dot_general x1, matrix products, body(): jnp.dot(masked.reshape(-1, lon_count), table, preferred_element_type=jnp....  21.6 us
    transpose x1, local copies, waits for them, and re-layouts, body(): block_rows = partial_sum.reshape(FIELDS, lat_band, lon_count // BLOCK, BL...  21.4 us
    ppermute x3, starting transfers between devices, with_halo(): lax.ppermute(head, axis, [((i + 1) % count, i) for i in range(ends)])  17 us
    reshape x1, local copies, waits for them, and re-layouts, body(): partial_sum.reshape(FIELDS, lat_band, lon_count // BLOCK, BLOCK)  16.2 us
  transfers between devices with their start and end apart: 9, of which 4 were waited for; matrix products, arithmetic and copies ran while one was open for 55% of the time, Pallas kernels for 0%

commit v1 on v0

--- a/solution.py
+++ b/solution.py
@@ -1,3 +1,4 @@
+import functools
 import math
 import jax
 import jax.numpy as jnp
@@ -9,6 +10,13 @@
 FULL_TURN = 2.0 * math.pi
 DIFFUSION = 0.2
 COUPLING = 0.5
+
+
+def _take_tails(local_values, mesh_ax):
+    return jnp.sum(lax.all_gather(local_values, mesh_ax), 0)
+
+
+convert_groups_on = functools.partial(_take_tails, mesh_ax="lev")
 
 
 def with_halo(cells, sides, width):
@@ -99,7 +107,7 @@
     arrived = (
         widened[:tile_count] + widened[2 * tile_count : 3 * tile_count] + widened[4 * tile_count :]
     )
-    tile_sums = lax.psum(arrived, "lev")
+    tile_sums = convert_groups_on(arrived)
     forcing = (
         tile_sums.reshape(ocean_rows, ocean_cols // BLOCK, FIELDS, BLOCK)
         .transpose(2, 0, 1, 3)

time: 346 us -> 323 us (0.934)
  waiting for transfers between devices: 40.2 us -> 20.1 us
    psum x1 -> x0, waiting for transfers between devices: 29.3 us -> none  [body(): tile_sums = lax.psum(arrived, 'lev')]
    all_to_all x1, waiting for transfers between devices: 0.01 us -> 6.74 us  [body(): lax.all_to_all(coeffs.transpose(4, 1, 0, 3, 2).reshape(wave_count, lev_de...]
    ppermute x3, starting transfers between devices: 17 us -> 12.5 us  [with_halo(): lax.ppermute(head, axis, [((i + 1) % count, i) for i in range(ends)])]
  transfers between devices with their start and end apart: 9 -> 9, of which waited for: 4 -> 5; matrix products, arithmetic and copies ran while one was open for 55% -> 14% of each run, Pallas kernels for 0% -> 0%
where the time goes in v1:
time: 323 us; the launch traced here: 322 us
  other arithmetic  117 us (36%)
  matrix products  70.4 us (22%)
  local copies, waits for them, and re-layouts  67 us (21%)
  starting transfers between devices  27.9 us (9%)
  waiting for transfers between devices  20.1 us (6%)
  between operations  14.5 us (4%)
  blocking collectives  5.55 us (2%)
    scatter-add x1, other arithmetic, body(): jax.ops.segment_sum(block_rows, every_slot, num_segments=3 * tile_count)  77.6 us
    dot_general x1, matrix products, body(): jnp.einsum('ql,qljk->qjk', column_weight, masked, preferred_element_type=...  43 us
    select_n x1, other arithmetic, body(): jnp.where(point_mask[None, None], atmos_fields, jnp.zeros((), jnp.bfloat16))  29.1 us
    transpose x1, local copies, waits for them, and re-layouts, body(): block_rows = partial_sum.reshape(FIELDS, lat_band, lon_count // BLOCK, BL...  21.4 us
    dot_general x1, matrix products, body(): jnp.dot(masked.reshape(-1, lon_count), table, preferred_element_type=jnp....  21.3 us
    reshape x1, local copies, waits for them, and re-layouts, body(): partial_sum.reshape(FIELDS, lat_band, lon_count // BLOCK, BLOCK)  16.3 us
    ppermute x3, starting transfers between devices, with_halo(): lax.ppermute(head, axis, [((i + 1) % count, i) for i in range(ends)])  12.5 us
    dot_general x1, local copies, waits for them, and re-layouts, body(): jnp.einsum('ql,qljk->qjk', column_weight, masked, preferred_element_type=...  11.2 us
  transfers between devices with their start and end apart: 9, of which 5 were waited for; matrix products, arithmetic and copies ran while one was open for 14% of the time, Pallas kernels for 0%

profile of v1, /device:TPU:4, one launch (start us, length us, event | category | flops | bytes accessed | tf_op | source)
XLA Modules:
  0.0 322.4 jit_solution(17510159955695285796)
XLA Ops:
  7.2 5.5 %all-gather.1 = s32[4,11,320]{2,1,0:T(8,128)S(1)} all-gather(s32[1,11,320]{2,1,0:T(8,128)} %bitcast.84), channel_id=1, replica_groups=mesh['lat'=2,'lev'=4,'ocn'=4] {'lev'}, dimensions={0}, use_global_device_ids=true | all-gather | bytes 70400 | tf_op jit(solution)/shard_map/all_gather | solution.py:98
  12.9 1.7 iota_compare_fusion
  14.6 0.1 copy.56
  14.7 0.2 rem.67
  15.0 0.2 div.38
  15.3 0.1 copy.55
  15.4 0.2 ne.124
  15.6 29.1 %broadcast_select_fusion = bf16[2,6,320,5632]{3,2,1,0:T(8,128)(2,1)} fusion(bf16[2,6,320,5632]{3,2,1,0:T(8,128)(2,1)} %param.9, pred[320,5632]{1,0:T(8,128)(4,1)S(1)} %iota_compare_fusion), kind=kLoop, calls=%fused_computation.6 | loop fusion | flops 21626880 | bytes 88309760 | tf_op jit(solution)/shard_map/jit(_where)/select_n | solution.py:62
  44.7 43.0 %fusion = f32[2,1,320,5632]{3,1,2,0:T(1,128)} fusion(bf16[2,6,320,5632]{3,2,1,0:T(8,128)(2,1)} %broadcast_select_fusion, bf16[2,6,1,1]{1,0,2,3:T(2,128)(2,1)S(1)} %bitcast.63), kind=kOutput, calls=%fused_computation.2 | convolution fusion | flops 43253760 | bytes 57671704 | tf_op jit(solution)/shard_map/ql,qljk->qjk/dot_general | solution.py:94
  87.7 11.2 %copy.82 = f32[2,1,320,5632]{3,2,0,1:T(8,128)} copy(f32[2,1,320,5632]{3,1,2,0:T(1,128)} %fusion) | data formatting | bytes 28835840 | tf_op jit(solution)/shard_map/ql,qljk->qjk/dot_general | solution.py:94
  98.9 16.3 %reshape.273 = f32[2,320,44,128]{3,2,1,0:T(8,128)} reshape(f32[2,320,5632]{2,1,0:T(8,128)} %bitcast.65) | data formatting | bytes 28835840 | tf_op jit(solution)/shard_map/reshape | solution.py:101
  115.1 21.4 %copy.58 = f32[320,44,2,128]{3,2,1,0:T(2,128)} copy(f32[320,44,2,128]{3,1,0,2:T(8,128)} %bitcast.64) | data formatting | bytes 28835840 | tf_op jit(solution)/shard_map/transpose | solution.py:102
  136.5 0.4 fusion.33
  136.9 77.6 %scatter_custom_fusion = f32[816,256]{1,0:T(8,128)S(1)} fusion(s32[14080]{0:T(1024)S(1)} %fusion.33, f32[1760,8,2,128]{3,2,1,0:T(2,128)} %bitcast.66, f32[]{:T(128)} %constant.51.clone.1), kind=kCustom, calls=%fused_computation.7 | custom fusion | flops 3604480 | bytes 15253508 | tf_op jit(solution)/shard_map/scatter-add | solution.py:105
  214.6 5.5 %collective-permute-start.3 = (f32[272,256]{1,0:T(8,128)S(1)}, f32[272,256]{1,0:T(8,128)S(1)}, u32[]{:S(2)}, u32[]{:S(2)}) collective-permute-start(f32[272,256]{1,0:T(8,128)S(1)} %get-tuple-element.23), channel_id=1, source_target_pairs={{1,0},{2,1},{3,2},{16,3},{17,16},{18,17},{19,18},{5,4},{6,5},{7,6}... | collective-permute-start | bytes 835592 | tf_op jit(solution)/shard_map/ppermute | solution.py:32
  220.0 1.9 collective-permute-start.2
  222.0 3.6 %cosine_convert_fusion = (bf16[5632,32]{0,1:T(8,128)(2,1)S(1)}, bf16[5632,32]{0,1:T(8,128)(2,1)S(1)}) fusion(s32[32]{0:T(128)S(1)} %copy-done.8), kind=kLoop, calls=%fused_computation.21 | loop fusion | flops 2162688 | bytes 721024 | tf_op jit(solution)/shard_map/convert
  225.7 1.3 collective-permute-done.3
  227.1 6.3 %collective-permute-done.2 = f32[272,256]{1,0:T(8,128)S(1)} collective-permute-done((f32[272,256]{1,0:T(8,128)S(1)}, f32[272,256]{1,0:T(8,128)S(1)}, u32[]{:S(2)}, u32[]{:S(2)}) %collective-permute-start.2) | collective-permute-done | bytes 278560 | tf_op jit(solution)/shard_map/ppermute | solution.py:30
  233.3 0.8 fusion.24
  234.1 21.3 %fusion.13 = bf16[32,6,2,2,320]{4,0,3,1,2:T(8,128)(2,1)S(1)} fusion(bf16[2,32,5632,1,1]{2,1,0,4,3:T(8,128)(2,1)S(1)} %bitcast.67, bf16[2,6,320,5632]{3,2,1,0:T(8,128)(2,1)} %broadcast_select_fusion, f32[32,320]{1,0:T(8,128)S(1)} %compare_select_fusion.2), kind=kOutput, calls=%fused_computation.15 | convolution fusion | flops 2768732160 | bytes 44507136 | tf_op jit(solution)/shard_map/dot_general | solution.py:70
  255.6 1.0 copy.53
  256.6 6.1 %all-to-all-start = ((bf16[32,24,320]{2,1,0:T(8,128)(2,1)}), bf16[32,24,320]{2,1,0:T(8,128)(2,1)S(1)}, u32[]{:S(2)}, u32[]{:S(2)}) async-start(bf16[32,24,320]{2,1,0:T(8,128)(2,1)} %copy.53), calls=%async_computation | async-start | bytes 1179648 | tf_op jit(solution)/shard_map/all_to_all | solution.py:73
  262.7 3.4 %collective-permute-start.1 = (f32[2,1,2176]{2,1,0:T(1,128)S(1)}, f32[2,1,2176]{2,1,0:T(1,128)S(1)}, u32[]{:S(2)}, u32[]{:S(2)}) collective-permute-start(f32[2,1,2176]{2,1,0:T(1,128)S(1)} %get-tuple-element.31), channel_id=1, source_target_pairs={{0,1},{1,2},{2,3},{3,16},{16,17},{17,18},{18,19},{4,5},{5,6},{6,7}... | collective-permute-start | bytes 52232 | tf_op jit(solution)/shard_map/ppermute | solution.py:30
  266.1 5.2 %collective-permute-start = (f32[2,1,2176]{2,1,0:T(1,128)S(1)}, f32[2,1,2176]{2,1,0:T(1,128)S(1)}, u32[]{:S(2)}, u32[]{:S(2)}) collective-permute-start(f32[2,1,2176]{2,1,0:T(1,128)S(1)} %get-tuple-element.30), channel_id=1, source_target_pairs={{1,0},{2,1},{3,2},{16,3},{17,16},{18,17},{19,18},{5,4},{6,5},{7,6}... | collective-permute-start | bytes 52232 | tf_op jit(solution)/shard_map/ppermute | solution.py:32
  271.5 0.2 rem.71
  271.7 0.1 copy.62
  271.8 0.2 div.40
  272.0 6.7 %all-to-all-done = bf16[32,24,320]{2,1,0:T(8,128)(2,1)S(1)} async-done(((bf16[32,24,320]{2,1,0:T(8,128)(2,1)}), bf16[32,24,320]{2,1,0:T(8,128)(2,1)S(1)}, u32[]{:S(2)}, u32[]{:S(2)}) %all-to-all-start) | async-done | bytes 491552 | tf_op jit(solution)/shard_map/all_to_all | solution.py:73
  278.8 0.2 copy.54
  279.0 1.2 all_to_all.16
  280.2 0.2 copy.60
  280.4 0.2 ne.132
  280.7 0.1 fusion.23
  281.1 1.4 reduce_sum.9
  282.5 0.1 reshape.275
  282.8 0.2 fusion.31
  283.0 0.7 slice_bitcast_fusion
  283.7 1.9 collective-permute-start.5
  285.6 3.9 %collective-permute-start.4 = (f32[16,2176]{1,0:T(8,128)S(1)}, f32[16,2176]{1,0:T(8,128)S(1)}, u32[]{:S(2)}, u32[]{:S(2)}) collective-permute-start(f32[16,2176]{1,0:T(8,128)S(1)} %get-tuple-element.25), channel_id=1, source_target_pairs={{0,1},{1,2},{2,3},{3,16},{16,17},{17,18},{18,19},{4,5},{5,6},{6,7}... | collective-permute-start | bytes 417800 | tf_op jit(solution)/shard_map/ppermute | solution.py:30
  289.5 1.1 collective-permute-done.5
  290.6 4.6 %collective-permute-done.4 = f32[16,2176]{1,0:T(8,128)S(1)} collective-permute-done((f32[16,2176]{1,0:T(8,128)S(1)}, f32[16,2176]{1,0:T(8,128)S(1)}, u32[]{:S(2)}, u32[]{:S(2)}) %collective-permute-start.4) | collective-permute-done | bytes 139296 | tf_op jit(solution)/shard_map/ppermute | solution.py:30
  295.3 5.9 %gather_fusion = f32[3520,128]{1,0:T(8,128)S(1)} fusion(f32[816,128]{1,0:T(8,128)S(1)} %reshape.277, s32[4096]{0:T(1024)S(1)} %pad_clamp_fusion), kind=kCustom, calls=%fused_computation | custom fusion | bytes 3618560 | tf_op jit(solution)/shard_map/jit(_take)/gather | solution.py:135
  301.2 1.6 gather.7
  302.7 2.2 copy.63
  305.0 1.7 select_select_fusion
  306.6 2.9 copy.64
  309.5 6.1 %fusion.46 = f32[4,96,384]{2,1,0:T(8,128)} fusion(bf16[4,96,2560]{2,1,0:T(8,128)(2,1)} %all-gather.5.cloned.1.call-done, bf16[4,2560,384]{2,1,0:T(8,128)(2,1)} %param.12), kind=kOutput, calls=%fused_computation.94 | convolution fusion | flops 754974720 | bytes 10420224 | tf_op jit(solution)/shard_map/srj,sjd->srd/dot_general | solution.py:80
  (53 shorter events, 1.3 us)
Async XLA Ops:
  7.2 37.6 %copy-start = (bf16[2,6]{1,0:T(2,128)(2,1)S(1)}, bf16[2,6]{1,0:T(2,128)(2,1)}, u32[]{:S(2)}) copy-start(bf16[2,6]{1,0:T(2,128)(2,1)} %param.13) | copy-start | bytes 76
  7.2 273.9 %all-gather.7.cloned.1.call-start = ((), (), s32[]{:S(2)}) async-start(), calls=%async_computation.2 | async-start | bytes 1392640 | tf_op jit(solution)/shard_map/all_gather | solution.py:16
  136.9 85.1 %copy-start.6 = (s32[320]{0:T(512)S(1)}, s32[320]{0:T(512)}, u32[]{:S(2)}) copy-start(s32[320]{0:T(512)} %param.10) | copy-start | bytes 3844
  136.9 85.1 %copy-start.8 = (s32[32]{0:T(128)S(1)}, s32[32]{0:T(128)}, u32[]{:S(2)}) copy-start(s32[32]{0:T(128)} %param.11) | copy-start | bytes 388
  214.6 12.5 %collective-permute-start.3 = (f32[272,256]{1,0:T(8,128)S(1)}, f32[272,256]{1,0:T(8,128)S(1)}, u32[]{:S(2)}, u32[]{:S(2)}) collective-permute-start(f32[272,256]{1,0:T(8,128)S(1)} %get-tuple-element.23), channel_id=1, source_target_pairs={{1,0},{2,1},{3,2},{16,3},{17,16},{18,17},{19,18},{5,4},{6,5},{7,6}... | collective-permute-start | bytes 835592 | tf_op jit(solution)/shard_map/ppermute | solution.py:32
  220.0 13.3 %collective-permute-start.2 = (f32[272,256]{1,0:T(8,128)S(1)}, f32[272,256]{1,0:T(8,128)S(1)}, u32[]{:S(2)}, u32[]{:S(2)}) collective-permute-start(f32[272,256]{1,0:T(8,128)S(1)} %get-tuple-element.22), channel_id=1, source_target_pairs={{0,1},{1,2},{2,3},{3,16},{16,17},{17,18},{18,19},{4,5},{5,6},{6,7}... | collective-permute-start | bytes 835592 | tf_op jit(solution)/shard_map/ppermute | solution.py:30
  234.1 28.6 %copy-start.2 = (f32[16,2176]{1,0:T(8,128)S(1)}, f32[16,2176]{1,0:T(8,128)}, u32[]{:S(2)}) copy-start(f32[16,2176]{1,0:T(8,128)} %param.15) | copy-start | bytes 417796
  234.1 28.6 %copy-start.3 = (f32[16,2176]{1,0:T(8,128)S(1)}, f32[16,2176]{1,0:T(8,128)}, u32[]{:S(2)}) copy-start(f32[16,2176]{1,0:T(8,128)} %param.16) | copy-start | bytes 417796
  234.1 37.2 %copy-start.5 = (s32[320,11]{0,1:T(8,128)S(1)}, s32[320,11]{0,1:T(8,128)}, u32[]{:S(2)}) copy-start(s32[320,11]{0,1:T(8,128)} %param.14) | copy-start | bytes 42244
  255.5 25.2 %copy-start.7 = (s32[16,17]{1,0:T(8,128)S(1)}, s32[16,17]{1,0:T(8,128)}, u32[]{:S(2)}) copy-start(s32[16,17]{1,0:T(8,128)} %param.17) | copy-start | bytes 3268
  256.6 22.2 %all-to-all-start = ((bf16[32,24,320]{2,1,0:T(8,128)(2,1)}), bf16[32,24,320]{2,1,0:T(8,128)(2,1)S(1)}, u32[]{:S(2)}, u32[]{:S(2)}) async-start(bf16[32,24,320]{2,1,0:T(8,128)(2,1)} %copy.53), calls=%async_computation | async-start | bytes 1179648 | tf_op jit(solution)/shard_map/all_to_all | solution.py:73
  262.7 46.8 %all-gather.5.cloned.1.call-start = ((), (), s32[]{:S(2)}) async-start(), calls=%async_computation.1 | async-start | bytes 2457600 | tf_op jit(solution)/shard_map/all_gather | solution.py:82
  262.7 20.0 %collective-permute-start.1 = (f32[2,1,2176]{2,1,0:T(1,128)S(1)}, f32[2,1,2176]{2,1,0:T(1,128)S(1)}, u32[]{:S(2)}, u32[]{:S(2)}) collective-permute-start(f32[2,1,2176]{2,1,0:T(1,128)S(1)} %get-tuple-element.31), channel_id=1, source_target_pairs={{0,1},{1,2},{2,3},{3,16},{16,17},{17,18},{18,19},{4,5},{5,6},{6,7}... | collective-permute-start | bytes 52232 | tf_op jit(solution)/shard_map/ppermute | solution.py:30
  266.1 16.6 %collective-permute-start = (f32[2,1,2176]{2,1,0:T(1,128)S(1)}, f32[2,1,2176]{2,1,0:T(1,128)S(1)}, u32[]{:S(2)}, u32[]{:S(2)}) collective-permute-start(f32[2,1,2176]{2,1,0:T(1,128)S(1)} %get-tuple-element.30), channel_id=1, source_target_pairs={{1,0},{2,1},{3,2},{16,3},{17,16},{18,17},{19,18},{5,4},{6,5},{7,6}... | collective-permute-start | bytes 52232 | tf_op jit(solution)/shard_map/ppermute | solution.py:32
  283.7 17.5 %copy-start.4 = (f32[16,2176]{1,0:T(8,128)}, f32[16,2176]{1,0:T(8,128)S(1)}, u32[]{:S(2)}) copy-start(f32[16,2176]{1,0:T(8,128)S(1)} %get-tuple-element.25) | copy-start | bytes 417796
  283.7 6.9 %collective-permute-start.5 = (f32[16,2176]{1,0:T(8,128)S(1)}, f32[16,2176]{1,0:T(8,128)S(1)}, u32[]{:S(2)}, u32[]{:S(2)}) collective-permute-start(f32[16,2176]{1,0:T(8,128)S(1)} %get-tuple-element.25), channel_id=1, source_target_pairs={{1,0},{2,1},{3,2},{16,3},{17,16},{18,17},{19,18},{5,4},{6,5},{7,6}... | collective-permute-start | bytes 417800 | tf_op jit(solution)/shard_map/ppermute | solution.py:32
  285.6 9.6 %collective-permute-start.4 = (f32[16,2176]{1,0:T(8,128)S(1)}, f32[16,2176]{1,0:T(8,128)S(1)}, u32[]{:S(2)}, u32[]{:S(2)}) collective-permute-start(f32[16,2176]{1,0:T(8,128)S(1)} %get-tuple-element.25), channel_id=1, source_target_pairs={{0,1},{1,2},{2,3},{3,16},{16,17},{17,18},{18,19},{4,5},{5,6},{6,7}... | collective-permute-start | bytes 417800 | tf_op jit(solution)/shard_map/ppermute | solution.py:30
  305.0 10.6 %copy-start.1 = (bf16[2,6]{1,0:T(2,128)(2,1)S(1)}, bf16[2,6]{1,0:T(2,128)(2,1)}, u32[]{:S(2)}) copy-start(bf16[2,6]{1,0:T(2,128)(2,1)} %param.13) | copy-start | bytes 76
Sparse Core Ops, SparseCore 0:
  234.2 18.0 all-gather.6
  280.3 20.0 all-gather.4
